TPU v7x, 32 devices: a whole 2x2x4 slice. The times are simulated.
32 devices in a mesh: sum: 8 (over z, x), mode: 4 (over y, core).
Axes of the slice: x: 2, y: 2, z: 4, core: 2. Of those that a mesh axis runs over, the one named last changes fastest.
Arguments:
- left_cores: bfloat16 [8, 512, 64, 512], P('sum', None, 'mode'), may hold values from -80 to 80, as said below
- right_cores: bfloat16 [8, 512, 64, 512], P('sum', None, 'mode'), may hold values from -6 to 6
- sketch: bfloat16 [64, 512, 512], P('mode'), may hold values from -0.03125 to 0.03125
Outputs:
- basis_core: float32 [512, 64, 512], P('sum', 'mode')
- carries: float32 [8, 512, 512], P('sum')
Inputs may be any that keep to these rules, and one draw needn't show every extreme that they name: `left_cores`: independent entries; each row (summand, left rank, mode index) has its own scale.
All inputs are finite; a program needn't handle non-finite values.
Results may differ from a plain program's by a relative error of at most 0.0035.
Values may be sent and summed in bfloat16 or wider, within the bound.
No kernel may reach another device: no remote copies, remote signals or barrier semaphores. Data moves between devices by JAX's collectives and lax.ppermute only.
A program may use at most 128 MiB of HBM per device.

v0:
```python
import math
import jax
import jax.numpy as jnp
from jax import lax
from jax.sharding import PartitionSpec as P

R_IN = 512
MODES = 64


def orthonormal(sketched, gram):
    lower = jnp.linalg.cholesky(gram)
    return lax.linalg.triangular_solve(
        lower, sketched, left_side=False, lower=True, transpose_a=True
    )


def per_device(left_cores, right_cores, sketch):
    sum_local, rows_in, mode_local, rank_width = left_cores.shape
    target = sketch.shape[2]
    flat_sketch = sketch.reshape(-1, target)
    flat_right = right_cores.reshape(sum_local * rank_width, -1)
    partial_map = jnp.dot(flat_right, flat_sketch, preferred_element_type=jnp.float32).reshape(
        sum_local, rank_width, target
    )
    mapped = lax.psum(partial_map, "mode").astype(jnp.bfloat16)
    flat_left = left_cores.reshape(sum_local, rows_in * mode_local, rank_width)
    local_sum = jnp.einsum("skr,srp->kp", flat_left, mapped, preferred_element_type=jnp.float32)
    local_sum = local_sum.reshape(rows_in, mode_local, target)
    factor = math.sqrt(R_IN * MODES)
    share = lax.psum_scatter(local_sum, "sum", scatter_dimension=0, tiled=True)
    flat_share = share.reshape(-1, target)
    gram_part = jnp.dot(flat_share.T, flat_share, precision=lax.Precision.HIGHEST)
    gram = lax.psum(gram_part, ("sum", "mode"))
    basis = orthonormal(flat_share, gram)
    block = basis.reshape(share.shape)
    rounded = block.astype(jnp.bfloat16)
    pieces = lax.all_gather(rounded, "sum", axis=0, tiled=True)
    count = pieces.shape[0]
    chosen = left_cores
    chosen = chosen.reshape(sum_local, count * mode_local, rank_width)
    partial_carry = jnp.einsum(
        "kp,skr->spr", pieces.reshape(-1, target), chosen, preferred_element_type=jnp.float32
    )
    carries = lax.psum(partial_carry, "mode")
    return (block * factor, carries)


def solution(mesh):
    in_specs = (P("sum", None, "mode", None), P("sum", None, "mode", None), P("mode", None, None))
    out_specs = (P("sum", "mode", None), P("sum", None, None))
    return jax.shard_map(
        per_device, mesh=mesh, in_specs=in_specs, out_specs=out_specs, check_vma=False
    )
```

profile of v0, /device:TPU:0, one launch (start us, length us, event | category | flops | bytes accessed | tf_op | source)
XLA Modules:
  0.0 864.9 jit_solution(7836462655036602845)
XLA Ops:
  7.2 16.4 %copy.36 = bf16[64,8,16,512]{3,1,2,0:T(8,128)(2,1)} copy(bf16[64,8,16,512]{3,2,1,0:T(8,128)(2,1)} %bitcast.87) | data formatting | bytes 16777216
  23.6 9.4 %convolution_bitcast_fusion.3 = f32[1,512,512]{2,1,0:T(8,128)S(1)} fusion(bf16[512,8192]{1,0:T(8,128)(2,1)} %bitcast.88, bf16[8192,512]{1,0:T(8,128)(2,1)} %bitcast.91), kind=kOutput, calls=%fused_computation.13 | convolution fusion | flops 4294967296 | bytes 17825792 | tf_op jit(solution)/shard_map/dot_general | solution.py:23
  33.0 28.2 %all-reduce.8 = bf16[1,512,512]{2,1,0:T(8,128)(2,1)S(1)} all-reduce(f32[1,512,512]{2,1,0:T(8,128)S(1)} %convolution_bitcast_fusion.3), channel_id=1, replica_groups=mesh['sum'=8,'mode'=4] {'mode'}, use_global_device_ids=true, to_apply=%region_0.0 | all-reduce | flops 262144 | bytes 1572864 | tf_op jit(solution)/shard_map/psum | solution.py:26
  61.2 27.3 %convolution_bitcast_fusion = f32[512,16,512]{0,2,1:T(8,128)} fusion(bf16[512,16,512]{2,1,0:T(8,128)(2,1)} %bitcast.81, bf16[1,512,512]{2,1,0:T(8,128)(2,1)S(1)} %all-reduce.8), kind=kOutput, calls=%fused_computation.2 | convolution fusion | flops 4294967296 | bytes 25690112 | tf_op jit(solution)/shard_map/skr,srp->kp/dot_general | solution.py:28
  88.6 20.2 %copy.23 = f32[512,16,512]{2,1,0:T(8,128)} copy(f32[512,16,512]{0,2,1:T(8,128)} %convolution_bitcast_fusion) | data formatting | bytes 33554432 | tf_op jit(solution)/shard_map/skr,srp->kp/dot_general | solution.py:28
  109.3 282.2 %reduce-scatter.2.cloned.1.call-done = f32[64,16,512]{2,1,0:T(8,128)} async-done(((f32[512,16,512]{2,1,0:T(8,128)}), f32[64,16,512]{2,1,0:T(8,128)}) %reduce-scatter.2.cloned.1.call-update) | async-done | bytes 2097168 | tf_op jit(solution)/shard_map/reduce_scatter | solution.py:31
  391.5 6.7 convolution_bitcast_fusion.2
  398.3 129.0 %all-reduce.5.cloned.1.call-done = f32[512,512]{0,1:T(8,128)} async-done(((f32[512,512]{0,1:T(8,128)}), f32[512,512]{0,1:T(8,128)}) %all-reduce.5.cloned.1.call-update) | async-done | bytes 1048592 | tf_op jit(solution)/shard_map/psum | solution.py:34
  527.3 1.6 copy.27
  529.2 1.0 copy-done.4
  530.2 11.7 %cholesky.104 = f32[128,128]{1,0:T(8,128)S(1)} custom-call(f32[128,128]{1,0:T(8,128)S(1)} %cholesky.266), custom_call_target="Cholesky" | custom-call | tf_op jit(solution)/shard_map/jit(cholesky)/cholesky | solution.py:12
  541.9 9.8 %custom-call.30 = f32[1,128,128]{1,2,0:T(8,128)S(1)} custom-call(f32[1,128,128]{2,1,0:T(8,128)S(1)} %get-tuple-element.31), custom_call_target="InvertDiagBlocksLowerTriangular" | custom-call | tf_op jit(solution)/shard_map/jit(cholesky)/cholesky | solution.py:12
  551.9 1.2 constant_dynamic-update-slice_fusion.3
  553.1 1.3 convolution_subtract_fusion.2
  554.4 11.7 %cholesky.217 = f32[128,128]{1,0:T(8,128)S(1)} custom-call(f32[128,128]{1,0:T(8,128)S(1)} %cholesky.270), custom_call_target="Cholesky" | custom-call | tf_op jit(solution)/shard_map/jit(cholesky)/cholesky | solution.py:12
  566.1 10.0 %custom-call.31 = f32[1,128,128]{1,2,0:T(8,128)S(1)} custom-call(f32[1,128,128]{2,1,0:T(8,128)S(1)} %get-tuple-element.28), custom_call_target="InvertDiagBlocksLowerTriangular" | custom-call | tf_op jit(solution)/shard_map/jit(cholesky)/cholesky | solution.py:12
  576.4 1.3 convolution_subtract_fusion.3
  577.7 11.7 %cholesky.238 = f32[128,128]{1,0:T(8,128)S(1)} custom-call(f32[128,128]{1,0:T(8,128)S(1)} %cholesky.275), custom_call_target="Cholesky" | custom-call | tf_op jit(solution)/shard_map/jit(cholesky)/cholesky | solution.py:12
  589.4 0.7 compare_reduce_fusion.1
  590.1 9.8 %custom-call.32 = f32[1,128,128]{1,2,0:T(8,128)S(1)} custom-call(f32[1,128,128]{2,1,0:T(8,128)S(1)} %get-tuple-element.25), custom_call_target="InvertDiagBlocksLowerTriangular" | custom-call | tf_op jit(solution)/shard_map/jit(cholesky)/cholesky | solution.py:12
  600.2 1.2 convolution_subtract_fusion.4
  601.4 11.7 %cholesky.255 = f32[128,128]{1,0:T(8,128)S(1)} custom-call(f32[128,128]{1,0:T(8,128)S(1)} %convolution_subtract_fusion.4), custom_call_target="Cholesky" | custom-call | tf_op jit(solution)/shard_map/jit(cholesky)/cholesky | solution.py:12
  613.1 0.6 compare_reduce_fusion
  613.8 0.7 compare_reduce_fusion.2
  617.0 1.3 select_select_fusion
  618.3 14.2 %while.1 = (s32[]{:T(128)}, f32[512,512]{1,0:T(8,128)}, s32[4,2]{0,1:T(2,128)S(1)}, f32[4,128,128]{2,1,0:T(8,128)}, s32[]{:T(128)}) while((s32[]{:T(128)}, f32[512,512]{1,0:T(8,128)}, s32[4,2]{0,1:T(2,128)S(1)}, f32[4,128,128]{2,1,0:T(8,128)}, s32[]{:T(128)}) %tuple.32), condition=%wide.while_cond, body=%wide.while_body.sunk | while | flops 2 | bytes 132705 | solution.py:13
  619.0 2.9 bitcast_dynamic-update-slice_fusion.2
  622.5 2.9 bitcast_dynamic-update-slice_fusion.2
  625.5 0.6 fusion.52
  626.1 2.9 bitcast_dynamic-update-slice_fusion.2
  629.0 0.6 fusion.52
  629.6 2.8 bitcast_dynamic-update-slice_fusion.2
  632.4 40.1 %custom-call.33 = f32[4,128,128]{1,2,0:T(8,128)S(1)} custom-call(f32[4,128,128]{2,1,0:T(8,128)} %get-tuple-element.9), custom_call_target="InvertDiagBlocksLowerTriangular" | custom-call | tf_op jit(solution)/shard_map/triangular_solve | solution.py:13
  672.6 0.6 fusion.16
  673.2 1.8 convolution_subtract_fusion.1
  675.0 0.6 fusion.30
  675.7 2.7 convolution_subtract_fusion
  678.4 0.6 fusion.29
  679.0 3.8 fusion.7
  682.9 0.6 fusion.28
  683.5 0.8 copy-done.2
  684.5 1.3 copy.29
  686.1 123.8 %all-gather.2.cloned.1.call-done = bf16[512,16,512]{2,1,0:T(8,128)(2,1)} async-done(((bf16[64,16,512]{2,1,0:T(8,128)(2,1)}), bf16[512,16,512]{2,1,0:T(8,128)(2,1)}) %all-gather.2.cloned.1.call-update) | async-done | bytes 8388624 | tf_op jit(solution)/shard_map/all_gather | solution.py:38
  809.9 11.2 %convolution_bitcast_fusion.1 = f32[1,512,512]{2,1,0:T(8,128)} fusion(bf16[8192,512]{1,0:T(8,128)(2,1)} %bitcast.92, bf16[8192,512]{1,0:T(8,128)(2,1)} %bitcast.82), kind=kOutput, calls=%fused_computation.11 | convolution fusion | flops 4294967296 | bytes 17825792 | tf_op jit(solution)/shard_map/kp,skr->spr/dot_general | solution.py:42
  821.2 1.5 fusion.11
  822.6 1.8 copy.28
  824.4 31.2 %all-reduce.7.cloned.1.call-done = f32[1,512,512]{2,1,0:T(8,128)} async-done(((f32[1,512,512]{2,1,0:T(8,128)}), f32[1,512,512]{2,1,0:T(8,128)}) %all-reduce.7.cloned.1.call-update) | async-done | bytes 1048592 | tf_op jit(solution)/shard_map/psum | solution.py:45
  855.6 2.3 copy.58
  (37 shorter events, 3.6 us)
Async XLA Ops:
  7.2 384.3 %reduce-scatter.2.cloned.1.call-start = ((), (), s32[]{:S(2)}) async-start(), calls=%async_computation.1 | async-start | bytes 18874368 | tf_op jit(solution)/shard_map/reduce_scatter | solution.py:31
  108.8 418.5 %all-reduce.5.cloned.1.call-start = ((), (), s32[]{:S(2)}) async-start(), calls=%async_computation.2 | async-start | bytes 2097152 | tf_op jit(solution)/shard_map/psum | solution.py:34
  398.2 411.7 %all-gather.2.cloned.1.call-start = ((), (), s32[]{:S(2)}) async-start(), calls=%async_computation.3 | async-start | bytes 9437184 | tf_op jit(solution)/shard_map/all_gather | solution.py:38
  527.3 1.7 copy-start.3
  529.2 1.0 copy-start.4
  577.6 94.9 %copy-start = (f32[64,16,512]{2,1,0:T(8,128)S(1)}, f32[64,16,512]{2,1,0:T(8,128)}, u32[]{:S(2)}) copy-start(f32[64,16,512]{2,1,0:T(8,128)} %reduce-scatter.2.cloned.1.call-done) | copy-start | bytes 6291460
  679.0 4.5 copy-start.1
  683.5 0.8 copy-start.2
  685.8 169.8 %all-reduce.7.cloned.1.call-start = ((), (), s32[]{:S(2)}) async-start(), calls=%async_computation.4 | async-start | bytes 2097152 | tf_op jit(solution)/shard_map/psum | solution.py:45
Sparse Core Ops, SparseCore 0:
  108.9 282.4 reduce-scatter.1
  398.3 128.9 all-reduce.4
  686.0 123.8 all-gather.1
  821.3 34.2 all-reduce.6
where the time goes:
time: 875 us; the launch traced here: 865 us
  waiting for transfers between devices  566 us (65%)
  other arithmetic  122 us (14%)
  matrix products  71.1 us (8%)
  local copies, waits for them, and re-layouts  59.7 us (7%)
  blocking collectives  28.2 us (3%)
  between operations  17 us (2%)
    reduce_scatter x1, waiting for transfers between devices, per_device(): share = lax.psum_scatter(local_sum, 'sum', scatter_dimension=0, tiled=True)  282 us
    psum x1, waiting for transfers between devices, per_device(): gram = lax.psum(gram_part, ('sum', 'mode'))  129 us
    all_gather x1, waiting for transfers between devices, per_device(): pieces = lax.all_gather(rounded, 'sum', axis=0, tiled=True)  124 us
    another operation x14, other arithmetic, orthonormal(): lower = jnp.linalg.cholesky(gram)  78.6 us
    another operation x3, other arithmetic, orthonormal(): lax.linalg.triangular_solve(lower, sketched, left_side=False, lower=True,...  41.4 us
    psum x1, waiting for transfers between devices, per_device(): carries = lax.psum(partial_carry, 'mode')  31.2 us
    psum x1, blocking collectives, per_device(): mapped = lax.psum(partial_map, 'mode').astype(jnp.bfloat16)  28.2 us
    dot_general x1, matrix products, per_device(): jnp.einsum('skr,srp->kp', flat_left, mapped, preferred_element_type=jnp.f...  27.3 us
  transfers between devices with their start and end apart: 4, of which 4 were waited for; matrix products, arithmetic and copies ran while one was open for 0% of the time, Pallas kernels for 0%

commit v1 on v0

--- a/solution.py
+++ b/solution.py
@@ -35,7 +35,22 @@
     basis = orthonormal(flat_share, gram)
     block = basis.reshape(share.shape)
     rounded = block.astype(jnp.bfloat16)
-    pieces = lax.all_gather(rounded, "sum", axis=0, tiled=True)
+    ways, here, step = (lax.axis_size("sum"), lax.axis_index("sum"), rounded.shape[0])
+    lengths = [n * ways if d == 0 else n for d, n in enumerate(rounded.shape)]
+    pieces = lax.dynamic_update_slice_in_dim(
+        jnp.zeros(lengths, rounded.dtype), rounded, here * step, axis=0
+    )
+    going_up = going_down = rounded
+    for far in range(1, ways // 2 + 1):
+        going_up = lax.ppermute(going_up, "sum", [(d, (d + 1) % ways) for d in range(ways)])
+        pieces = lax.dynamic_update_slice_in_dim(
+            pieces, going_up, (here - far) % ways * step, axis=0
+        )
+        if 2 * far < ways:
+            going_down = lax.ppermute(going_down, "sum", [(d, (d - 1) % ways) for d in range(ways)])
+            pieces = lax.dynamic_update_slice_in_dim(
+                pieces, going_down, (here + far) % ways * step, axis=0
+            )
     count = pieces.shape[0]
     chosen = left_cores
     chosen = chosen.reshape(sum_local, count * mode_local, rank_width)

time: 875 us -> 913 us (1.043)
  waiting for transfers between devices: 566 us -> 585 us
  starting transfers between devices: 0.82 us -> 17.6 us
    ppermute x0 -> x7, waiting for transfers between devices: none -> 141 us  [the longest x4 141 us: per_device(): lax.ppermute(going_up, 'sum', [(d, (d + 1) % ways) for d in range(ways)])]
    all_gather x1 -> x0, waiting for transfers between devices: 124 us -> none  [per_device(): pieces = lax.all_gather(rounded, 'sum', axis=0, tiled=True)]
    ppermute x0 -> x7, starting transfers between devices: none -> 17 us  [the longest x4 9.29 us: per_device(): lax.ppermute(going_up, 'sum', [(d, (d + 1) % ways) for d in range(ways)])]
    unnamed x12 -> x22, local copies, waits for them, and re-layouts: 20.4 us -> 20.5 us
  transfers between devices with their start and end apart: 4 -> 10, of which waited for: 4 -> 7; matrix products, arithmetic and copies ran while one was open for 0% -> 1% of each run, Pallas kernels for 0% -> 0%
where the time goes in v1:
time: 913 us; the launch traced here: 903 us
  waiting for transfers between devices  585 us (64%)
  other arithmetic  123 us (13%)
  local copies, waits for them, and re-layouts  66.1 us (7%)
  matrix products  65.3 us (7%)
  blocking collectives  28.2 us (3%)
  starting transfers between devices  17.6 us (2%)
  between operations  17.1 us (2%)
    reduce_scatter x1, waiting for transfers between devices, per_device(): share = lax.psum_scatter(local_sum, 'sum', scatter_dimension=0, tiled=True)  283 us
    ppermute x4, waiting for transfers between devices, per_device(): lax.ppermute(going_up, 'sum', [(d, (d + 1) % ways) for d in range(ways)])  141 us
    psum x1, waiting for transfers between devices, per_device(): gram = lax.psum(gram_part, ('sum', 'mode'))  129 us
    another operation x14, other arithmetic, orthonormal(): lower = jnp.linalg.cholesky(gram)  78.6 us
    another operation x3, other arithmetic, orthonormal(): lax.linalg.triangular_solve(lower, sketched, left_side=False, lower=True,...  41.4 us
    psum x1, waiting for transfers between devices, per_device(): carries = lax.psum(partial_carry, 'mode')  32.2 us
    psum x1, blocking collectives, per_device(): mapped = lax.psum(partial_map, 'mode').astype(jnp.bfloat16)  28.2 us
    dot_general x1, matrix products, per_device(): jnp.einsum('skr,srp->kp', flat_left, mapped, preferred_element_type=jnp.f...  27.3 us
  transfers between devices with their start and end apart: 10, of which 7 were waited for; matrix products, arithmetic and copies ran while one was open for 1% of the time, Pallas kernels for 0%

profile of v1, /device:TPU:0, one launch (start us, length us, event | category | flops | bytes accessed | tf_op | source)
XLA Modules:
  0.0 902.6 jit_solution(8924212241882664668)
XLA Ops:
  7.2 16.4 %copy.36 = bf16[64,8,16,512]{3,1,2,0:T(8,128)(2,1)} copy(bf16[64,8,16,512]{3,2,1,0:T(8,128)(2,1)} %bitcast.89) | data formatting | bytes 16777216
  23.6 9.4 %convolution_bitcast_fusion.3 = f32[1,512,512]{2,1,0:T(8,128)S(1)} fusion(bf16[512,8192]{1,0:T(8,128)(2,1)} %bitcast.91, bf16[8192,512]{1,0:T(8,128)(2,1)} %bitcast.96), kind=kOutput, calls=%fused_computation.13 | convolution fusion | flops 4294967296 | bytes 17825792 | tf_op jit(solution)/shard_map/dot_general | solution.py:23
  33.0 28.2 %all-reduce.8 = bf16[1,512,512]{2,1,0:T(8,128)(2,1)S(1)} all-reduce(f32[1,512,512]{2,1,0:T(8,128)S(1)} %convolution_bitcast_fusion.3), channel_id=1, replica_groups=mesh['sum'=8,'mode'=4] {'mode'}, use_global_device_ids=true, to_apply=%region_0.0 | all-reduce | flops 262144 | bytes 1572864 | tf_op jit(solution)/shard_map/psum | solution.py:26
  61.2 27.3 %convolution_bitcast_fusion = f32[512,16,512]{0,2,1:T(8,128)} fusion(bf16[512,16,512]{2,1,0:T(8,128)(2,1)} %bitcast.81, bf16[1,512,512]{2,1,0:T(8,128)(2,1)S(1)} %all-reduce.8), kind=kOutput, calls=%fused_computation.2 | convolution fusion | flops 4294967296 | bytes 25690112 | tf_op jit(solution)/shard_map/skr,srp->kp/dot_general | solution.py:28
  88.5 20.2 %copy.23 = f32[512,16,512]{2,1,0:T(8,128)} copy(f32[512,16,512]{0,2,1:T(8,128)} %convolution_bitcast_fusion) | data formatting | bytes 33554432 | tf_op jit(solution)/shard_map/skr,srp->kp/dot_general | solution.py:28
  109.2 282.8 %reduce-scatter.2.cloned.1.call-done = f32[64,16,512]{2,1,0:T(8,128)} async-done(((f32[512,16,512]{2,1,0:T(8,128)}), f32[64,16,512]{2,1,0:T(8,128)}) %reduce-scatter.2.cloned.1.call-update) | async-done | bytes 2097168 | tf_op jit(solution)/shard_map/reduce_scatter | solution.py:31
  392.1 6.8 convolution_bitcast_fusion.2
  398.9 128.9 %all-reduce.5.cloned.1.call-done = f32[512,512]{0,1:T(8,128)} async-done(((f32[512,512]{0,1:T(8,128)}), f32[512,512]{0,1:T(8,128)}) %all-reduce.5.cloned.1.call-update) | async-done | bytes 1048592 | tf_op jit(solution)/shard_map/psum | solution.py:34
  527.8 1.6 copy.27
  529.3 1.4 fusion.15
  531.8 11.7 %cholesky.104 = f32[128,128]{1,0:T(8,128)S(1)} custom-call(f32[128,128]{1,0:T(8,128)S(1)} %cholesky.266), custom_call_target="Cholesky" | custom-call | tf_op jit(solution)/shard_map/jit(cholesky)/cholesky | solution.py:12
  543.5 9.8 %custom-call.30 = f32[1,128,128]{1,2,0:T(8,128)S(1)} custom-call(f32[1,128,128]{2,1,0:T(8,128)S(1)} %get-tuple-element.31), custom_call_target="InvertDiagBlocksLowerTriangular" | custom-call | tf_op jit(solution)/shard_map/jit(cholesky)/cholesky | solution.py:12
  556.0 11.7 %cholesky.217 = f32[128,128]{1,0:T(8,128)S(1)} custom-call(f32[128,128]{1,0:T(8,128)S(1)} %cholesky.270), custom_call_target="Cholesky" | custom-call | tf_op jit(solution)/shard_map/jit(cholesky)/cholesky | solution.py:12
  567.7 10.0 %custom-call.31 = f32[1,128,128]{1,2,0:T(8,128)S(1)} custom-call(f32[1,128,128]{2,1,0:T(8,128)S(1)} %get-tuple-element.28), custom_call_target="InvertDiagBlocksLowerTriangular" | custom-call | tf_op jit(solution)/shard_map/jit(cholesky)/cholesky | solution.py:12
  578.0 1.3 convolution_subtract_fusion.3
  579.3 11.7 %cholesky.238 = f32[128,128]{1,0:T(8,128)S(1)} custom-call(f32[128,128]{1,0:T(8,128)S(1)} %cholesky.275), custom_call_target="Cholesky" | custom-call | tf_op jit(solution)/shard_map/jit(cholesky)/cholesky | solution.py:12
  591.7 9.8 %custom-call.32 = f32[1,128,128]{1,2,0:T(8,128)S(1)} custom-call(f32[1,128,128]{2,1,0:T(8,128)S(1)} %get-tuple-element.25), custom_call_target="InvertDiagBlocksLowerTriangular" | custom-call | tf_op jit(solution)/shard_map/jit(cholesky)/cholesky | solution.py:12
  602.9 11.7 %cholesky.255 = f32[128,128]{1,0:T(8,128)S(1)} custom-call(f32[128,128]{1,0:T(8,128)S(1)} %convolution_subtract_fusion.4), custom_call_target="Cholesky" | custom-call | tf_op jit(solution)/shard_map/jit(cholesky)/cholesky | solution.py:12
  618.5 1.3 select_select_fusion
  619.8 13.7 %while.1 = (s32[]{:T(128)}, f32[512,512]{1,0:T(8,128)}, s32[4,2]{0,1:T(2,128)S(1)}, f32[4,128,128]{2,1,0:T(8,128)}, s32[]{:T(128)}) while((s32[]{:T(128)}, f32[512,512]{1,0:T(8,128)}, s32[4,2]{0,1:T(2,128)S(1)}, f32[4,128,128]{2,1,0:T(8,128)}, s32[]{:T(128)}) %tuple.32), condition=%wide.while_cond, body=%wide.while_body.sunk | while | flops 2 | bytes 132705 | solution.py:13
  620.5 2.8 bitcast_dynamic-update-slice_fusion.2
  623.9 2.8 bitcast_dynamic-update-slice_fusion.2
  627.3 2.8 bitcast_dynamic-update-slice_fusion.2
  630.8 2.8 bitcast_dynamic-update-slice_fusion.2
  633.5 40.1 %custom-call.33 = f32[4,128,128]{1,2,0:T(8,128)S(1)} custom-call(f32[4,128,128]{2,1,0:T(8,128)} %get-tuple-element.9), custom_call_target="InvertDiagBlocksLowerTriangular" | custom-call | tf_op jit(solution)/shard_map/triangular_solve | solution.py:13
  674.3 1.8 convolution_subtract_fusion.1
  676.8 2.7 convolution_subtract_fusion
  680.1 3.8 fusion.7
  686.1 1.5 collective-permute-start
  687.7 3.3 collective-permute-start.1
  690.9 40.8 %collective-permute-done = bf16[64,16,512]{2,1,0:T(8,128)(2,1)S(1)} collective-permute-done((bf16[64,16,512]{2,1,0:T(8,128)(2,1)S(1)}, bf16[64,16,512]{2,1,0:T(8,128)(2,1)S(1)}, u32[]{:S(2)}, u32[]{:S(2)}) %collective-permute-start) | collective-permute-done | bytes 1048608 | tf_op jit(solution)/shard_map/ppermute | solution.py:45
  731.7 2.5 collective-permute-start.2
  734.2 2.2 collective-permute-start.3
  736.4 41.7 %collective-permute-done.2 = bf16[64,16,512]{2,1,0:T(8,128)(2,1)S(1)} collective-permute-done((bf16[64,16,512]{2,1,0:T(8,128)(2,1)S(1)}, bf16[64,16,512]{2,1,0:T(8,128)(2,1)S(1)}, u32[]{:S(2)}, u32[]{:S(2)}) %collective-permute-start.2) | collective-permute-done | bytes 1048608 | tf_op jit(solution)/shard_map/ppermute | solution.py:45
  778.1 2.5 collective-permute-start.4
  780.6 2.2 collective-permute-start.5
  782.9 41.8 %collective-permute-done.4 = bf16[64,16,512]{2,1,0:T(8,128)(2,1)} collective-permute-done((bf16[64,16,512]{2,1,0:T(8,128)(2,1)S(1)}, bf16[64,16,512]{2,1,0:T(8,128)(2,1)}, u32[]{:S(2)}, u32[]{:S(2)}) %collective-permute-start.4) | collective-permute-done | bytes 1048608 | tf_op jit(solution)/shard_map/ppermute | solution.py:45
  824.6 2.8 collective-permute-start.6
  829.1 1.6 constant_dynamic-update-slice_fusion.3
  830.7 1.9 constant_dynamic-update-slice_fusion.2
  832.6 1.3 constant_dynamic-update-slice_fusion.1
  833.9 17.1 %collective-permute-done.6 = bf16[64,16,512]{2,1,0:T(8,128)(2,1)} collective-permute-done((bf16[64,16,512]{2,1,0:T(8,128)(2,1)}, bf16[64,16,512]{2,1,0:T(8,128)(2,1)}, u32[]{:S(2)}, u32[]{:S(2)}) %collective-permute-start.6) | collective-permute-done | bytes 1048608 | tf_op jit(solution)/shard_map/ppermute | solution.py:45
  851.0 1.3 constant_dynamic-update-slice_fusion
  852.4 5.5 convolution_bitcast_fusion.1
  857.9 1.4 fusion.11
  859.3 1.8 copy.28
  861.1 32.2 %all-reduce.7.cloned.1.call-done = f32[1,512,512]{2,1,0:T(8,128)} async-done(((f32[1,512,512]{2,1,0:T(8,128)}), f32[1,512,512]{2,1,0:T(8,128)}) %all-reduce.7.cloned.1.call-update) | async-done | bytes 1048592 | tf_op jit(solution)/shard_map/psum | solution.py:60
  893.3 2.3 copy.64
  (68 shorter events, 16.1 us)
Async XLA Ops:
  7.2 384.9 %reduce-scatter.2.cloned.1.call-start = ((), (), s32[]{:S(2)}) async-start(), calls=%async_computation.1 | async-start | bytes 18874368 | tf_op jit(solution)/shard_map/reduce_scatter | solution.py:31
  108.8 419.0 %all-reduce.5.cloned.1.call-start = ((), (), s32[]{:S(2)}) async-start(), calls=%async_computation.2 | async-start | bytes 2097152 | tf_op jit(solution)/shard_map/psum | solution.py:34
  398.8 274.9 %copy-start = (f32[64,16,512]{2,1,0:T(8,128)S(1)}, f32[64,16,512]{2,1,0:T(8,128)}, u32[]{:S(2)}) copy-start(f32[64,16,512]{2,1,0:T(8,128)} %reduce-scatter.2.cloned.1.call-done) | copy-start | bytes 6291460
  398.8 494.5 %all-reduce.7.cloned.1.call-start = ((), (), s32[]{:S(2)}) async-start(), calls=%async_computation.3 | async-start | bytes 2097152 | tf_op jit(solution)/shard_map/psum | solution.py:60
  530.8 1.0 copy-start.3
  680.1 4.5 copy-start.1
  684.6 0.8 copy-start.2
  686.1 45.5 %collective-permute-start = (bf16[64,16,512]{2,1,0:T(8,128)(2,1)S(1)}, bf16[64,16,512]{2,1,0:T(8,128)(2,1)S(1)}, u32[]{:S(2)}, u32[]{:S(2)}) collective-permute-start(bf16[64,16,512]{2,1,0:T(8,128)(2,1)S(1)} %bitcast.92), channel_id=1, source_target_pairs={{0,4},{4,8},{8,12},{12,16},{16,20},{20,24},{24,28},{28,0},{1,5},{5... | collective-permute-start | bytes 3145736 | tf_op jit(solution)/shard_map/ppermute | solution.py:45
  687.7 46.5 %collective-permute-start.1 = (bf16[64,16,512]{2,1,0:T(8,128)(2,1)S(1)}, bf16[64,16,512]{2,1,0:T(8,128)(2,1)S(1)}, u32[]{:S(2)}, u32[]{:S(2)}) collective-permute-start(bf16[64,16,512]{2,1,0:T(8,128)(2,1)S(1)} %bitcast.93), channel_id=1, source_target_pairs={{0,28},{4,0},{8,4},{12,8},{16,12},{20,16},{24,20},{28,24},{1,29},{... | collective-permute-start | bytes 3145736 | tf_op jit(solution)/shard_map/ppermute | solution.py:50
  731.7 46.4 %collective-permute-start.2 = (bf16[64,16,512]{2,1,0:T(8,128)(2,1)S(1)}, bf16[64,16,512]{2,1,0:T(8,128)(2,1)S(1)}, u32[]{:S(2)}, u32[]{:S(2)}) collective-permute-start(bf16[64,16,512]{2,1,0:T(8,128)(2,1)S(1)} %collective-permute-done), channel_id=1, source_target_pairs={{0,4},{4,8},{8,12},{12,16},{16,20},{20,24},{24,28},{28,0},{1,5},{5... | collective-permute-start | bytes 3145736 | tf_op jit(solution)/shard_map/ppermute | solution.py:45
  734.2 44.0 %copy-start.4 = (bf16[64,16,512]{2,1,0:T(8,128)(2,1)}, bf16[64,16,512]{2,1,0:T(8,128)(2,1)S(1)}, u32[]{:S(2)}) copy-start(bf16[64,16,512]{2,1,0:T(8,128)(2,1)S(1)} %collective-permute-done.1) | copy-start | bytes 3145732
  734.2 46.4 %collective-permute-start.3 = (bf16[64,16,512]{2,1,0:T(8,128)(2,1)S(1)}, bf16[64,16,512]{2,1,0:T(8,128)(2,1)}, u32[]{:S(2)}, u32[]{:S(2)}) collective-permute-start(bf16[64,16,512]{2,1,0:T(8,128)(2,1)S(1)} %collective-permute-done.1), channel_id=1, source_target_pairs={{0,28},{4,0},{8,4},{12,8},{16,12},{20,16},{24,20},{28,24},{1,29},{... | collective-permute-start | bytes 3145736 | tf_op jit(solution)/shard_map/ppermute | solution.py:50
  778.1 2.5 copy-start.6
  778.1 46.5 %collective-permute-start.4 = (bf16[64,16,512]{2,1,0:T(8,128)(2,1)S(1)}, bf16[64,16,512]{2,1,0:T(8,128)(2,1)}, u32[]{:S(2)}, u32[]{:S(2)}) collective-permute-start(bf16[64,16,512]{2,1,0:T(8,128)(2,1)S(1)} %collective-permute-done.2), channel_id=1, source_target_pairs={{0,4},{4,8},{8,12},{12,16},{16,20},{20,24},{24,28},{28,0},{1,5},{5... | collective-permute-start | bytes 3145736 | tf_op jit(solution)/shard_map/ppermute | solution.py:45
  780.6 52.0 %collective-permute-start.5 = (bf16[64,16,512]{2,1,0:T(8,128)(2,1)}, bf16[64,16,512]{2,1,0:T(8,128)(2,1)}, u32[]{:S(2)}, u32[]{:S(2)}) collective-permute-start(bf16[64,16,512]{2,1,0:T(8,128)(2,1)} %collective-permute-done.3), channel_id=1, source_target_pairs={{0,28},{4,0},{8,4},{12,8},{16,12},{20,16},{24,20},{28,24},{1,29},{... | collective-permute-start | bytes 3145736 | tf_op jit(solution)/shard_map/ppermute | solution.py:50
  824.6 26.4 %collective-permute-start.6 = (bf16[64,16,512]{2,1,0:T(8,128)(2,1)}, bf16[64,16,512]{2,1,0:T(8,128)(2,1)}, u32[]{:S(2)}, u32[]{:S(2)}) collective-permute-start(bf16[64,16,512]{2,1,0:T(8,128)(2,1)} %collective-permute-done.4), channel_id=1, source_target_pairs={{0,4},{4,8},{8,12},{12,16},{16,20},{20,24},{24,28},{28,0},{1,5},{5... | collective-permute-start | bytes 3145736 | tf_op jit(solution)/shard_map/ppermute | solution.py:45
  827.5 1.3 copy-start.5
  827.5 1.5 copy-start.7
  828.5 23.8 %slice-start = ((s8[8388608]{0:T(1024)(128)(4,1)}), s8[4194304]{0:T(1024)(128)(4,1)S(1)}, s32[]{:S(2)}) async-start(s8[8388608]{0:T(1024)(128)(4,1)} %bitcast.82), calls=%async_computation.4 | async-start | bytes 8388608
  829.1 23.2 %slice-start.1 = ((s8[8388608]{0:T(1024)(128)(4,1)}), s8[4194304]{0:T(1024)(128)(4,1)S(1)}, s32[]{:S(2)}) async-start(s8[8388608]{0:T(1024)(128)(4,1)} %bitcast.82), calls=%async_computation.5 | async-start | bytes 8388608
Sparse Core Ops, SparseCore 0:
  108.9 283.1 reduce-scatter.1
  399.0 128.7 all-reduce.4
  858.0 35.2 all-reduce.6
